TPU v7x, 32 devices: a whole 2x2x4 slice. The times are simulated.
32 devices in a mesh: box: 8 (over z, y), rep: 4 (over x, core).
Axes of the slice: x: 2, y: 2, z: 4, core: 2. Of those that a mesh axis runs over, the one named last changes fastest.
Arguments:
- targets: float32 [128, 256], P('box'), may hold values from -6 to 6
- noise_var: float32 [128, 256], P('box'), may hold values from 1 to 4
- near_tiles: bfloat16 [128, 8, 256, 256], P('box', 'rep'), may hold values from -1 to 1
- near_partners: int32 [128, 8], P('box', 'rep'), may hold values from -1 to 127, as said below
- leaf_bases: bfloat16 [128, 64, 256], P('box'), may hold values from -0.375 to 0.375
- transfer: bfloat16 [128, 64, 64], P('box'), may hold values from -0.375 to 0.375
- parents: int32 [128], P('box'), may hold values from 0 to 31, as said below
- coupling: bfloat16 [160, 16, 64, 64], P('box', 'rep'), may hold values from -0.109375 to 0.109375
- coupling_partners: int32 [160, 16], P('box', 'rep'), may hold values from -1 to 159, as said below
Outputs:
- weights: float32 [128, 256], P('box')
- residual: float32 [128, 256], P('box')
Inputs may be any that keep to these rules, and one draw needn't show every extreme that they name: `near_partners`: the first slot of each box's row is the box itself; every other entry is -1 or a box at most 16 boxes after the row's box. `coupling_partners`: each entry is -1 or a node of the same level as the row's node (leaf box or parent) with a higher number. The parents of the boxes of one index of box are that index's 4 parents. Along those boxes the parent number never decreases, so each parent's children are one contiguous run of one box or more.
All inputs are finite; a program needn't handle non-finite values.
Results may differ from a plain program's by a relative error of at most 0.006.
Values may be sent and summed in bfloat16 or wider, within the bound.
No kernel may reach another device: no remote copies, remote signals or barrier semaphores. Data moves between devices by JAX's collectives and lax.ppermute only.
A program may use at most 64 MiB of HBM per device.

v0:
```python
import jax
import jax.numpy as jnp
from jax import lax
from jax.sharding import PartitionSpec as P

ITERS = 2


def shifted(shard, axis, by):
    devices = lax.axis_size(axis)
    pairs = [(i, i + by) for i in range(devices) if 0 <= i + by < devices]
    return lax.ppermute(shard, axis, pairs)


def local(
    targets,
    noise_var,
    near_tiles,
    near_partners,
    leaf_bases,
    transfer,
    parents,
    coupling,
    coupling_partners,
):
    box_count = targets.shape[0]
    node_count = coupling.shape[0]
    group_count = node_count - box_count
    rank_width = coupling.shape[2]
    box_rank = lax.axis_index("box")
    all_nodes = lax.axis_size("box") * node_count
    near_valid = near_partners >= 0
    near_local = jnp.where(near_valid, near_partners - box_rank * box_count, 0)
    near_onehot = (
        (jnp.arange(2 * box_count, dtype=jnp.int32)[:, None] == near_local.reshape(1, -1))
        & near_valid.reshape(1, -1)
    ).astype(jnp.float32)
    parent_local = parents - box_rank * group_count
    parent_onehot = (
        jnp.arange(group_count, dtype=jnp.int32)[:, None] == parent_local[None, :]
    ).astype(jnp.float32)
    far_valid = coupling_partners >= 0
    far_index = jnp.where(far_valid, coupling_partners, 0)
    bf_zero = jnp.zeros((), jnp.bfloat16)

    def squares(vector):
        return lax.psum(jnp.sum(vector * vector), "box")

    weights = jnp.zeros_like(targets)
    residual = targets
    direction = targets
    norm_now = squares(residual)
    for iteration in range(ITERS):
        rounded = direction.astype(jnp.bfloat16)
        following = shifted(rounded, "box", -1)
        extended = jnp.concatenate([rounded, following], axis=0)
        near_in = jnp.where(near_valid[:, :, None], extended[near_local], bf_zero)
        forward = jnp.einsum(
            "bsij,bsj->bi", near_tiles, near_in, preferred_element_type=jnp.float32
        )
        mirrored = jnp.einsum(
            "bsij,bi->bsj", near_tiles, rounded, preferred_element_type=jnp.float32
        )
        landed = jnp.dot(
            near_onehot, mirrored.reshape(-1, mirrored.shape[2]), precision=lax.Precision.HIGHEST
        )
        arrived = shifted(landed[box_count:], "box", 1)
        near_part = forward + landed[:box_count] + arrived
        leaf_coef = jnp.einsum(
            "brl,bl->br", leaf_bases, rounded, preferred_element_type=jnp.float32
        ).astype(jnp.bfloat16)
        upward = jnp.einsum("brq,br->bq", transfer, leaf_coef, preferred_element_type=jnp.float32)
        group_coef = jnp.dot(parent_onehot, upward, precision=lax.Precision.HIGHEST).astype(
            jnp.bfloat16
        )
        node_coef = jnp.concatenate([leaf_coef, group_coef], axis=0)
        every_coef = lax.all_gather(node_coef, "box", axis=0, tiled=True)
        partner_coef = jnp.where(far_valid[:, :, None], every_coef[far_index], bf_zero)
        far_forward = jnp.einsum(
            "nsab,nsb->na", coupling, partner_coef, preferred_element_type=jnp.float32
        )
        far_mirror = jnp.einsum(
            "nsab,na->nsb", coupling, node_coef, preferred_element_type=jnp.float32
        )
        far_mirror = far_mirror * far_valid[:, :, None].astype(jnp.float32)
        spread = (
            jnp.zeros((all_nodes, rank_width), jnp.float32)
            .at[far_index.reshape(-1)]
            .add(far_mirror.reshape(-1, rank_width))
        )
        node_sums = lax.psum_scatter(spread, "box", scatter_dimension=0, tiled=True)
        near_total, far_total = lax.psum((near_part, node_sums + far_forward), "rep")
        group_out = far_total[box_count:].astype(jnp.bfloat16)
        from_parent = jnp.einsum(
            "brq,bq->br", transfer, group_out[parent_local], preferred_element_type=jnp.float32
        )
        downward = (far_total[:box_count] + from_parent).astype(jnp.bfloat16)
        far_field = jnp.einsum(
            "brl,br->bl", leaf_bases, downward, preferred_element_type=jnp.float32
        )
        image_vec = noise_var * direction + near_total + far_field
        step_size = norm_now / lax.psum(jnp.sum(direction * image_vec), "box")
        weights = weights + step_size * direction
        residual = residual - step_size * image_vec
        norm_next = squares(residual)
        direction = residual + norm_next / norm_now * direction
        norm_now = norm_next
    return (weights, residual)


def solution(mesh):
    placed = (
        P("box", None),
        P("box", None),
        P("box", "rep", None, None),
        P("box", "rep"),
        P("box", None, None),
        P("box", None, None),
        P("box"),
        P("box", "rep", None, None),
        P("box", "rep"),
    )
    return jax.shard_map(
        local,
        mesh=mesh,
        in_specs=placed,
        out_specs=(P("box", None), P("box", None)),
        check_vma=False,
    )
```

profile of v0, /device:TPU:0, one launch (start us, length us, event | category | flops | bytes accessed | tf_op | source)
XLA Modules:
  0.0 256.1 jit_solution(12259696300122468750)
XLA Ops:
  0.7 0.9 convert_bitcast_fusion.1
  1.6 2.8 %fusion.22 = f32[16,1,2,256]{3,1,2,0:T(1,128)S(1)} fusion(bf16[16,2,256,256]{3,2,1,0:T(8,128)(2,1)} %param.11, bf16[16,256,1,1]{1,0,2,3:T(8,128)(2,1)S(1)} %convert_bitcast_fusion.1), kind=kOutput, calls=%fused_computation.46 | convolution fusion | flops 4194304 | bytes 4235264 | tf_op jit(solution)/shard_map/bsij,bi->bsj/dot_general | solution.py:61
  4.9 0.1 fusion.27
  5.1 4.9 %collective-permute-start.1 = (f32[16,256]{1,0:T(8,128)S(1)}, f32[16,256]{1,0:T(8,128)S(1)}, u32[]{:S(2)}, u32[]{:S(2)}) collective-permute-start(f32[16,256]{1,0:T(8,128)S(1)} %slice.47), channel_id=1, source_target_pairs={{0,4},{4,8},{8,12},{12,16},{16,20},{20,24},{24,28},{1,5},{5,9},{9,... | collective-permute-start | bytes 49160 | tf_op jit(solution)/shard_map/ppermute | solution.py:12
  10.0 1.3 collective-permute-start
  11.3 0.2 fusion.20
  12.0 0.2 fusion.45
  12.2 0.1 convolution_convert_fusion.1
  12.3 0.3 fusion.31
  12.7 0.9 scatter_custom_fusion
  13.6 39.5 %all-reduce = f32[160,64]{1,0:T(8,128)S(1)} all-reduce(f32[160,64]{1,0:T(8,128)S(1)} %scatter_custom_fusion), channel_id=2, replica_groups=mesh['box'=8,'rep'=4] {'box'}, use_global_device_ids=true, to_apply=%region_4.5.clone | all-reduce | flops 10240 | bytes 81920
  53.1 30.7 %all-gather = bf16[8,20,64]{2,1,0:T(8,128)(2,1)S(1)} all-gather(bf16[1,20,64]{2,1,0:T(8,128)(2,1)S(1)} %get-tuple-element.23), channel_id=1, replica_groups=mesh['box'=8,'rep'=4] {'box'}, dimensions={0}, use_global_device_ids=true | all-gather | bytes 23040 | tf_op jit(solution)/shard_map/all_gather | solution.py:77
  84.0 0.7 gather_fusion.1
  84.8 0.4 fusion.2
  85.3 0.1 reshape.64
  85.4 0.6 dynamic-slice
  86.7 0.6 gather_fusion
  87.5 3.4 %fusion.10 = f32[16,1,256,1]{2,1,3,0:T(1,128)S(1)} fusion(bf16[16,2,256,256]{3,2,1,0:T(8,128)(2,1)} %param.11, bf16[16,2,256,1]{2,1,0,3:T(2,128)(2,1)S(1)} %fusion.12), kind=kOutput, calls=%fused_computation.22 | convolution fusion | flops 4194304 | bytes 4227072 | tf_op jit(solution)/shard_map/bsij,bsj->bi/dot_general | solution.py:58
  90.9 10.3 %all-reduce.4 = (f32[20,64]{1,0:T(8,128)S(1)}, f32[16,256]{1,0:T(8,128)S(1)}) all-reduce(f32[20,64]{1,0:T(8,128)S(1)} %dynamic-slice_add_fusion.1, f32[16,256]{1,0:T(8,128)S(1)} %fusion.15), channel_id=1, replica_groups=mesh['box'=8,'rep'=4] {'rep'}, use_global_device_ids=true, to_apply=%region_5.6 | all-reduce | flops 5376 | bytes 43008 | tf_op jit(solution)/shard_map/psum | solution.py:92
  101.2 0.6 gather_fusion.2
  101.7 0.2 fusion.43
  102.0 0.2 fusion.41
  102.2 0.6 multiply_reduce_fusion.2
  102.8 17.8 %all-reduce.2 = (f32[]{:T(128)}, f32[]{:T(128)}) all-reduce(f32[]{:T(128)} %get-tuple-element.3, f32[]{:T(128)} %get-tuple-element.2), channel_id=1, replica_groups=mesh['box'=8,'rep'=4] {'box'}, use_global_device_ids=true, to_apply=%region_1.2 | all-reduce | flops 2 | bytes 16 | tf_op jit(solution)/shard_map/psum | solution.py:47
  121.9 0.6 multiply_reduce_fusion.1
  122.5 19.7 %psum.60 = f32[]{:T(128)} all-reduce(f32[]{:T(128)} %get-tuple-element.10), channel_id=1, replica_groups=mesh['box'=8,'rep'=4] {'box'}, use_global_device_ids=true, to_apply=%region_9.10 | all-reduce | flops 1 | bytes 8 | tf_op jit(solution)/shard_map/psum | solution.py:47
  143.6 0.2 fusion.16
  143.9 1.3 collective-permute-start.2
  145.2 0.2 fusion.39
  145.3 0.1 convolution_convert_fusion
  145.5 0.3 fusion.29
  145.9 0.9 scatter_custom_fusion.1
  146.7 36.4 %all-reduce.1 = f32[160,64]{1,0:T(8,128)S(1)} all-reduce(f32[160,64]{1,0:T(8,128)S(1)} %scatter_custom_fusion.1), channel_id=3, replica_groups=mesh['box'=8,'rep'=4] {'box'}, use_global_device_ids=true, to_apply=%region_12.13.clone | all-reduce | flops 10240 | bytes 81920
  183.2 30.7 %all-gather.1 = bf16[8,20,64]{2,1,0:T(8,128)(2,1)S(1)} all-gather(bf16[1,20,64]{2,1,0:T(8,128)(2,1)S(1)} %get-tuple-element.21), channel_id=1, replica_groups=mesh['box'=8,'rep'=4] {'box'}, dimensions={0}, use_global_device_ids=true | all-gather | bytes 23040 | tf_op jit(solution)/shard_map/all_gather | solution.py:77
  213.9 0.7 gather_fusion.4
  214.6 0.4 fusion
  215.0 2.9 %fusion.18 = f32[16,1,2,256]{3,1,2,0:T(1,128)S(1)} fusion(bf16[16,2,256,256]{3,2,1,0:T(8,128)(2,1)} %param.11, bf16[16,256,1,1]{1,0,2,3:T(8,128)(2,1)S(1)} %bitcast.105), kind=kOutput, calls=%fused_computation.42 | convolution fusion | flops 4194304 | bytes 4235264 | tf_op jit(solution)/shard_map/bsij,bi->bsj/dot_general | solution.py:61
  218.0 0.1 fusion.25
  218.1 1.3 collective-permute-start.3
  219.5 0.6 gather_fusion.3
  220.2 3.4 %fusion.8 = f32[16,1,256,1]{2,1,3,0:T(1,128)S(1)} fusion(bf16[16,2,256,256]{3,2,1,0:T(8,128)(2,1)} %param.11, bf16[16,2,256,1]{2,1,0,3:T(2,128)(2,1)S(1)} %fusion.13), kind=kOutput, calls=%fused_computation.19 | convolution fusion | flops 4194304 | bytes 4227072 | tf_op jit(solution)/shard_map/bsij,bsj->bi/dot_general | solution.py:58
  223.6 10.3 %all-reduce.3 = (f32[20,64]{1,0:T(8,128)S(1)}, f32[16,256]{1,0:T(8,128)S(1)}) all-reduce(f32[20,64]{1,0:T(8,128)S(1)} %dynamic-slice_add_fusion, f32[16,256]{1,0:T(8,128)S(1)} %fusion.14), channel_id=1, replica_groups=mesh['box'=8,'rep'=4] {'rep'}, use_global_device_ids=true, to_apply=%region_13.14 | all-reduce | flops 5376 | bytes 43008 | tf_op jit(solution)/shard_map/psum | solution.py:92
  233.9 0.6 gather_fusion.5
  234.5 0.2 fusion.37
  234.7 0.2 fusion.35
  234.9 0.6 multiply_reduce_fusion
  235.5 18.6 %psum.63 = f32[]{:T(128)} all-reduce(f32[]{:T(128)} %multiply_reduce_fusion), channel_id=1, replica_groups=mesh['box'=8,'rep'=4] {'box'}, use_global_device_ids=true, to_apply=%region_15.16 | all-reduce | flops 1 | bytes 8 | tf_op jit(solution)/shard_map/psum | solution.py:102
  255.5 0.6 multiply_subtract_fusion
  (77 shorter events, 2.0 us)
Async XLA Ops:
  0.6 11.7 %copy-start = (bf16[20,4,64,64]{3,2,1,0:T(8,128)(2,1)S(1)}, bf16[20,4,64,64]{3,2,1,0:T(8,128)(2,1)}, u32[]{:S(2)}) copy-start(bf16[20,4,64,64]{3,2,1,0:T(8,128)(2,1)} %param.16) | copy-start | bytes 1966084
  0.6 9.3 %copy-start.2 = (f32[16,256]{1,0:T(8,128)S(1)}, f32[16,256]{1,0:T(8,128)}, u32[]{:S(2)}) copy-start(f32[16,256]{1,0:T(8,128)} %param.9) | copy-start | bytes 49156
  0.7 3.8 %copy-start.5 = (s32[16,2]{0,1:T(2,128)S(1)}, s32[16,2]{0,1:T(2,128)}, u32[]{:S(2)}) copy-start(s32[16,2]{0,1:T(2,128)} %param.12) | copy-start | bytes 388
  0.7 10.6 %copy-start.1 = (bf16[16,64,256]{2,1,0:T(8,128)(2,1)S(1)}, bf16[16,64,256]{2,1,0:T(8,128)(2,1)}, u32[]{:S(2)}) copy-start(bf16[16,64,256]{2,1,0:T(8,128)(2,1)} %param.13) | copy-start | bytes 1572868
  0.7 10.9 %copy-start.4 = (s32[20,4]{0,1:T(4,128)S(1)}, s32[20,4]{0,1:T(4,128)}, u32[]{:S(2)}) copy-start(s32[20,4]{0,1:T(4,128)} %param.17) | copy-start | bytes 964
  0.7 11.3 %copy-start.7 = (bf16[16,64,64]{2,1,0:T(8,128)(2,1)S(1)}, bf16[16,64,64]{2,1,0:T(8,128)(2,1)}, u32[]{:S(2)}) copy-start(bf16[16,64,64]{2,1,0:T(8,128)(2,1)} %param.14) | copy-start | bytes 393220
  0.7 11.5 %copy-start.6 = (s32[16]{0:T(128)S(1)}, s32[16]{0:T(128)}, u32[]{:S(2)}) copy-start(s32[16]{0:T(128)} %param.15) | copy-start | bytes 196
  1.6 83.9 %copy-start.8 = (u32[32]{0:T(128)S(1)}, u32[32]{0:T(128)}, u32[]{:S(2)}) copy-start(u32[32]{0:T(128)} %constant.33) | copy-start | bytes 388
  5.1 85.8 %collective-permute-start.1 = (f32[16,256]{1,0:T(8,128)S(1)}, f32[16,256]{1,0:T(8,128)S(1)}, u32[]{:S(2)}, u32[]{:S(2)}) collective-permute-start(f32[16,256]{1,0:T(8,128)S(1)} %slice.47), channel_id=1, source_target_pairs={{0,4},{4,8},{8,12},{12,16},{16,20},{20,24},{24,28},{1,5},{5,9},{9,... | collective-permute-start | bytes 49160 | tf_op jit(solution)/shard_map/ppermute | solution.py:12
  10.0 76.8 %collective-permute-start = (bf16[16,256]{1,0:T(8,128)(2,1)S(1)}, bf16[16,256]{1,0:T(8,128)(2,1)S(1)}, u32[]{:S(2)}, u32[]{:S(2)}) collective-permute-start(bf16[16,256]{1,0:T(8,128)(2,1)S(1)} %convert_element_type.33), channel_id=1, source_target_pairs={{4,0},{8,4},{12,8},{16,12},{20,16},{24,20},{28,24},{5,1},{9,5},{13... | collective-permute-start | bytes 24584 | tf_op jit(solution)/shard_map/ppermute | solution.py:12
  12.6 89.6 %copy-start.3 = (f32[16,256]{1,0:T(8,128)S(1)}, f32[16,256]{1,0:T(8,128)}, u32[]{:S(2)}) copy-start(f32[16,256]{1,0:T(8,128)} %param.10) | copy-start | bytes 49156
  143.9 75.6 %collective-permute-start.2 = (bf16[16,256]{1,0:T(8,128)(2,1)S(1)}, bf16[16,256]{1,0:T(8,128)(2,1)S(1)}, u32[]{:S(2)}, u32[]{:S(2)}) collective-permute-start(bf16[16,256]{1,0:T(8,128)(2,1)S(1)} %fusion.57), channel_id=1, source_target_pairs={{4,0},{8,4},{12,8},{16,12},{20,16},{24,20},{28,24},{5,1},{9,5},{13... | collective-permute-start | bytes 24584 | tf_op jit(solution)/shard_map/ppermute | solution.py:12
  218.1 5.5 %collective-permute-start.3 = (f32[16,256]{1,0:T(8,128)S(1)}, f32[16,256]{1,0:T(8,128)S(1)}, u32[]{:S(2)}, u32[]{:S(2)}) collective-permute-start(f32[16,256]{1,0:T(8,128)S(1)} %slice.51), channel_id=1, source_target_pairs={{0,4},{4,8},{8,12},{12,16},{16,20},{20,24},{24,28},{1,5},{5,9},{9,... | collective-permute-start | bytes 49160 | tf_op jit(solution)/shard_map/ppermute | solution.py:12
where the time goes:
time: 257 us; the launch traced here: 256 us
  blocking collectives  214 us (83%)
  matrix products  16.1 us (6%)
  starting transfers between devices  8.75 us (3%)
  between operations  5.83 us (2%)
  other arithmetic  5.8 us (2%)
  local copies, waits for them, and re-layouts  5.68 us (2%)
    unnamed x2, blocking collectives  76 us
    all_gather x2, blocking collectives, local(): every_coef = lax.all_gather(node_coef, 'box', axis=0, tiled=True)  61.3 us
    psum x2, blocking collectives, squares(): return lax.psum(jnp.sum(vector * vector), 'box')  37.5 us
    psum x2, blocking collectives, local(): lax.psum((near_part, node_sums + far_forward), 'rep')  20.6 us
    psum x1, blocking collectives, local(): step_size = norm_now / lax.psum(jnp.sum(direction * image_vec), 'box')  18.6 us
    ppermute x4, starting transfers between devices, shifted(): return lax.ppermute(shard, axis, pairs)  8.75 us
    dot_general x2, matrix products, local(): jnp.einsum('bsij,bsj->bi', near_tiles, near_in, preferred_element_type=jn...  6.73 us
    dot_general x2, matrix products, local(): jnp.einsum('bsij,bi->bsj', near_tiles, rounded, preferred_element_type=jn...  5.7 us
  transfers between devices with their start and end apart: 4, of which 0 were waited for; matrix products, arithmetic and copies ran while one was open for 7% of the time, Pallas kernels for 0%

commit v1 on v0

--- a/solution.py
+++ b/solution.py
@@ -74,7 +74,22 @@
             jnp.bfloat16
         )
         node_coef = jnp.concatenate([leaf_coef, group_coef], axis=0)
-        every_coef = lax.all_gather(node_coef, "box", axis=0, tiled=True)
+        passed = lax.psum(1, "box")
+        odd = lax.axis_index("box")
+        res, n_now, main = (passed, odd, node_coef.shape[0])
+        piece_out, block_now = (node_coef, 1)
+        while block_now < res:
+            piece_out = jnp.concatenate(
+                [
+                    piece_out,
+                    lax.ppermute(
+                        piece_out, "box", [(idx, (idx - block_now) % res) for idx in range(res)]
+                    ),
+                ],
+                axis=0,
+            )
+            block_now = 2 * block_now
+        every_coef = jnp.roll(piece_out, n_now * main, axis=0)
         partner_coef = jnp.where(far_valid[:, :, None], every_coef[far_index], bf_zero)
         far_forward = jnp.einsum(
             "nsab,nsb->na", coupling, partner_coef, preferred_element_type=jnp.float32

time: 257 us -> 210 us (0.82)
  blocking collectives: 214 us -> 147 us
  starting transfers between devices: 8.75 us -> 19.4 us
  waiting for transfers between devices: 0.01 us -> 4.28 us
  other arithmetic: 5.8 us -> 8.88 us
    all_gather x2 -> x0, blocking collectives: 61.3 us -> none  [local(): every_coef = lax.all_gather(node_coef, 'box', axis=0, tiled=True)]
    ppermute x0 -> x6, starting transfers between devices: none -> 11 us  [local(): lax.ppermute(piece_out, 'box', [(idx, (idx - block_now) % res) for idx in...]
    unnamed x2, blocking collectives: 76 us -> 70.8 us
    ppermute x0 -> x6, waiting for transfers between devices: none -> 4.27 us  [local(): lax.ppermute(piece_out, 'box', [(idx, (idx - block_now) % res) for idx in...]
  transfers between devices with their start and end apart: 4 -> 10, of which waited for: 0 -> 3; matrix products, arithmetic and copies ran while one was open for 7% -> 10% of each run, Pallas kernels for 0% -> 0%
where the time goes in v1:
time: 210 us; the launch traced here: 209 us
  blocking collectives  147 us (70%)
  starting transfers between devices  19.4 us (9%)
  matrix products  18 us (9%)
  other arithmetic  8.88 us (4%)
  local copies, waits for them, and re-layouts  5.94 us (3%)
  between operations  5.85 us (3%)
  waiting for transfers between devices  4.28 us (2%)
    unnamed x2, blocking collectives  70.8 us
    psum x2, blocking collectives, squares(): return lax.psum(jnp.sum(vector * vector), 'box')  37.5 us
    psum x2, blocking collectives, local(): lax.psum((near_part, node_sums + far_forward), 'rep')  20.6 us
    psum x1, blocking collectives, local(): step_size = norm_now / lax.psum(jnp.sum(direction * image_vec), 'box')  17.7 us
    ppermute x6, starting transfers between devices, local(): lax.ppermute(piece_out, 'box', [(idx, (idx - block_now) % res) for idx in...  11 us
    ppermute x4, starting transfers between devices, shifted(): return lax.ppermute(shard, axis, pairs)  8.42 us
    dot_general x2, matrix products, local(): jnp.einsum('bsij,bsj->bi', near_tiles, near_in, preferred_element_type=jn...  6.73 us
    dot_general x2, matrix products, local(): jnp.einsum('bsij,bi->bsj', near_tiles, rounded, preferred_element_type=jn...  5.68 us
  transfers between devices with their start and end apart: 10, of which 3 were waited for; matrix products, arithmetic and copies ran while one was open for 10% of the time, Pallas kernels for 0%

profile of v1, /device:TPU:0, one launch (start us, length us, event | category | flops | bytes accessed | tf_op | source)
XLA Modules:
  0.0 209.0 jit_solution(8238365426744272782)
XLA Ops:
  0.7 0.8 convert_bitcast_fusion.3
  1.5 1.3 fusion.22
  2.8 0.7 compare_select_fusion.2
  3.5 1.1 fusion.47
  4.7 6.1 %collective-permute-start.2 = (bf16[20,64]{1,0:T(8,128)(2,1)S(1)}, bf16[20,64]{1,0:T(8,128)(2,1)S(1)}, u32[]{:S(2)}, u32[]{:S(2)}) collective-permute-start(bf16[20,64]{1,0:T(8,128)(2,1)S(1)} %get-tuple-element.24), channel_id=1, source_target_pairs={{0,28},{4,0},{8,4},{12,8},{16,12},{20,16},{24,20},{28,24},{1,29},{... | collective-permute-start | bytes 7688 | tf_op jit(solution)/shard_map/ppermute | solution.py:85
  10.8 0.7 convert_bitcast_fusion.1
  11.5 0.7 broadcast_compare_fusion.1
  12.2 0.7 compare_select_fusion.1
  13.3 2.8 %fusion.24 = f32[16,1,2,256]{3,1,2,0:T(1,128)S(1)} fusion(bf16[16,2,256,256]{3,2,1,0:T(8,128)(2,1)} %param.13, bf16[16,256,1,1]{1,0,2,3:T(8,128)(2,1)S(1)} %convert_bitcast_fusion.1), kind=kOutput, calls=%fused_computation.54 | convolution fusion | flops 4194304 | bytes 4235264 | tf_op jit(solution)/shard_map/bsij,bi->bsj/dot_general | solution.py:61
  16.3 1.3 collective-permute-start.1
  17.6 1.3 collective-permute-start
  19.7 0.3 fusion.33
  20.1 0.9 scatter_custom_fusion
  21.0 4.7 %collective-permute-start.3 = (bf16[40,64]{1,0:T(8,128)(2,1)S(1)}, bf16[40,64]{1,0:T(8,128)(2,1)S(1)}, u32[]{:S(2)}, u32[]{:S(2)}) collective-permute-start(bf16[40,64]{1,0:T(8,128)(2,1)S(1)} %pad_maximum_fusion.4), channel_id=1, source_target_pairs={{0,24},{4,28},{8,0},{12,4},{16,8},{20,12},{24,16},{28,20},{1,25},{... | collective-permute-start | bytes 15368 | tf_op jit(solution)/shard_map/ppermute | solution.py:85
  25.7 33.9 %all-reduce = f32[160,64]{1,0:T(8,128)S(1)} all-reduce(f32[160,64]{1,0:T(8,128)S(1)} %scatter_custom_fusion), channel_id=2, replica_groups=mesh['box'=8,'rep'=4] {'box'}, use_global_device_ids=true, to_apply=%region_4.5.clone | all-reduce | flops 10240 | bytes 81920
  59.7 0.6 dynamic-slice
  61.1 0.6 gather_fusion
  61.8 3.4 %fusion.12 = f32[16,1,256,1]{2,1,3,0:T(1,128)S(1)} fusion(bf16[16,2,256,256]{3,2,1,0:T(8,128)(2,1)} %param.13, bf16[16,2,256,1]{2,1,0,3:T(2,128)(2,1)S(1)} %fusion.14), kind=kOutput, calls=%fused_computation.28 | convolution fusion | flops 4194304 | bytes 4227072 | tf_op jit(solution)/shard_map/bsij,bsj->bi/dot_general | solution.py:58
  65.2 0.5 collective-permute-done.4
  66.1 0.7 gather_fusion.1
  66.8 0.4 fusion.4
  67.3 10.3 %all-reduce.4 = (f32[20,64]{1,0:T(8,128)S(1)}, f32[16,256]{1,0:T(8,128)S(1)}) all-reduce(f32[20,64]{1,0:T(8,128)S(1)} %dynamic-slice_add_fusion.1, f32[16,256]{1,0:T(8,128)S(1)} %fusion.17), channel_id=1, replica_groups=mesh['box'=8,'rep'=4] {'rep'}, use_global_device_ids=true, to_apply=%region_5.7 | all-reduce | flops 5376 | bytes 43008 | tf_op jit(solution)/shard_map/psum | solution.py:107
  77.6 0.6 gather_fusion.2
  78.2 0.2 fusion.45
  78.4 0.2 fusion.43
  78.6 0.6 multiply_reduce_fusion.2
  79.2 19.8 %all-reduce.2 = (f32[]{:T(128)}, f32[]{:T(128)}) all-reduce(f32[]{:T(128)} %get-tuple-element.4, f32[]{:T(128)} %get-tuple-element.3), channel_id=1, replica_groups=mesh['box'=8,'rep'=4] {'box'}, use_global_device_ids=true, to_apply=%region_1.2 | all-reduce | flops 2 | bytes 16 | tf_op jit(solution)/shard_map/psum | solution.py:47
  100.3 0.6 multiply_reduce_fusion.1
  100.9 17.7 %psum.60 = f32[]{:T(128)} all-reduce(f32[]{:T(128)} %get-tuple-element.11), channel_id=1, replica_groups=mesh['box'=8,'rep'=4] {'box'}, use_global_device_ids=true, to_apply=%region_9.11 | all-reduce | flops 1 | bytes 8 | tf_op jit(solution)/shard_map/psum | solution.py:47
  120.0 1.3 collective-permute-start.5
  121.3 0.2 fusion.18
  121.6 2.9 %fusion.20 = f32[16,1,2,256]{3,1,2,0:T(1,128)S(1)} fusion(bf16[16,2,256,256]{3,2,1,0:T(8,128)(2,1)} %param.13, bf16[16,256,1,1]{1,0,2,3:T(8,128)(2,1)S(1)} %bitcast.101), kind=kOutput, calls=%fused_computation.50 | convolution fusion | flops 4194304 | bytes 4235264 | tf_op jit(solution)/shard_map/bsij,bi->bsj/dot_general | solution.py:61
  124.6 4.5 %collective-permute-start.6 = (f32[16,256]{1,0:T(8,128)S(1)}, f32[16,256]{1,0:T(8,128)S(1)}, u32[]{:S(2)}, u32[]{:S(2)}) collective-permute-start(f32[16,256]{1,0:T(8,128)S(1)} %slice.51), channel_id=1, source_target_pairs={{0,4},{4,8},{8,12},{12,16},{16,20},{20,24},{24,28},{1,5},{5,9},{9,... | collective-permute-start | bytes 49160 | tf_op jit(solution)/shard_map/ppermute | solution.py:12
  129.6 0.3 fusion.31
  130.0 0.9 scatter_custom_fusion.1
  130.8 3.3 %collective-permute-done.7 = bf16[20,64]{1,0:T(8,128)(2,1)S(1)} collective-permute-done((bf16[20,64]{1,0:T(8,128)(2,1)S(1)}, bf16[20,64]{1,0:T(8,128)(2,1)S(1)}, u32[]{:S(2)}, u32[]{:S(2)}) %collective-permute-start.7) | collective-permute-done | bytes 2592 | tf_op jit(solution)/shard_map/ppermute | solution.py:85
  134.2 36.9 %all-reduce.1 = f32[160,64]{1,0:T(8,128)S(1)} all-reduce(f32[160,64]{1,0:T(8,128)S(1)} %scatter_custom_fusion.1), channel_id=3, replica_groups=mesh['box'=8,'rep'=4] {'box'}, use_global_device_ids=true, to_apply=%region_12.14.clone | all-reduce | flops 10240 | bytes 81920
  171.2 0.6 gather_fusion.3
  171.9 3.4 %fusion.10 = f32[16,1,256,1]{2,1,3,0:T(1,128)S(1)} fusion(bf16[16,2,256,256]{3,2,1,0:T(8,128)(2,1)} %param.13, bf16[16,2,256,1]{2,1,0,3:T(2,128)(2,1)S(1)} %fusion.15), kind=kOutput, calls=%fused_computation.25 | convolution fusion | flops 4194304 | bytes 4227072 | tf_op jit(solution)/shard_map/bsij,bsj->bi/dot_general | solution.py:58
  175.3 0.5 collective-permute-done.9
  176.2 0.7 gather_fusion.4
  176.9 0.4 fusion.2
  177.4 10.3 %all-reduce.3 = (f32[20,64]{1,0:T(8,128)S(1)}, f32[16,256]{1,0:T(8,128)S(1)}) all-reduce(f32[20,64]{1,0:T(8,128)S(1)} %dynamic-slice_add_fusion, f32[16,256]{1,0:T(8,128)S(1)} %fusion.16), channel_id=1, replica_groups=mesh['box'=8,'rep'=4] {'rep'}, use_global_device_ids=true, to_apply=%region_13.15 | all-reduce | flops 5376 | bytes 43008 | tf_op jit(solution)/shard_map/psum | solution.py:107
  187.7 0.6 gather_fusion.5
  188.3 0.2 fusion.39
  188.7 0.6 multiply_reduce_fusion
  189.3 17.7 %psum.63 = f32[]{:T(128)} all-reduce(f32[]{:T(128)} %multiply_reduce_fusion), channel_id=1, replica_groups=mesh['box'=8,'rep'=4] {'box'}, use_global_device_ids=true, to_apply=%region_15.17 | all-reduce | flops 1 | bytes 8 | tf_op jit(solution)/shard_map/psum | solution.py:117
  208.4 0.6 multiply_subtract_fusion
  (89 shorter events, 3.9 us)
Async XLA Ops:
  0.6 19.0 %copy-start = (bf16[20,4,64,64]{3,2,1,0:T(8,128)(2,1)S(1)}, bf16[20,4,64,64]{3,2,1,0:T(8,128)(2,1)}, u32[]{:S(2)}) copy-start(bf16[20,4,64,64]{3,2,1,0:T(8,128)(2,1)} %param.18) | copy-start | bytes 1966084
  0.6 59.1 %copy-start.6 = (u32[32]{0:T(128)S(1)}, u32[32]{0:T(128)}, u32[]{:S(2)}) copy-start(u32[32]{0:T(128)} %constant.49) | copy-start | bytes 388
  0.7 17.0 %copy-start.2 = (f32[16,256]{1,0:T(8,128)S(1)}, f32[16,256]{1,0:T(8,128)}, u32[]{:S(2)}) copy-start(f32[16,256]{1,0:T(8,128)} %param.11) | copy-start | bytes 49156
  0.7 18.3 %copy-start.4 = (s32[20,4]{0,1:T(4,128)S(1)}, s32[20,4]{0,1:T(4,128)}, u32[]{:S(2)}) copy-start(s32[20,4]{0,1:T(4,128)} %param.19) | copy-start | bytes 964
  4.7 16.2 %collective-permute-start.2 = (bf16[20,64]{1,0:T(8,128)(2,1)S(1)}, bf16[20,64]{1,0:T(8,128)(2,1)S(1)}, u32[]{:S(2)}, u32[]{:S(2)}) collective-permute-start(bf16[20,64]{1,0:T(8,128)(2,1)S(1)} %get-tuple-element.24), channel_id=1, source_target_pairs={{0,28},{4,0},{8,4},{12,8},{16,12},{20,16},{24,20},{28,24},{1,29},{... | collective-permute-start | bytes 7688 | tf_op jit(solution)/shard_map/ppermute | solution.py:85
  16.3 48.9 %collective-permute-start.1 = (f32[16,256]{1,0:T(8,128)S(1)}, f32[16,256]{1,0:T(8,128)S(1)}, u32[]{:S(2)}, u32[]{:S(2)}) collective-permute-start(f32[16,256]{1,0:T(8,128)S(1)} %slice.47), channel_id=1, source_target_pairs={{0,4},{4,8},{8,12},{12,16},{16,20},{20,24},{24,28},{1,5},{5,9},{9,... | collective-permute-start | bytes 49160 | tf_op jit(solution)/shard_map/ppermute | solution.py:12
  17.6 43.4 %collective-permute-start = (bf16[16,256]{1,0:T(8,128)(2,1)S(1)}, bf16[16,256]{1,0:T(8,128)(2,1)S(1)}, u32[]{:S(2)}, u32[]{:S(2)}) collective-permute-start(bf16[16,256]{1,0:T(8,128)(2,1)S(1)} %convert_element_type.33), channel_id=1, source_target_pairs={{4,0},{8,4},{12,8},{16,12},{20,16},{24,20},{28,24},{5,1},{9,5},{13... | collective-permute-start | bytes 24584 | tf_op jit(solution)/shard_map/ppermute | solution.py:12
  19.1 59.0 %copy-start.5 = (bf16[16,64,64]{2,1,0:T(8,128)(2,1)S(1)}, bf16[16,64,64]{2,1,0:T(8,128)(2,1)}, u32[]{:S(2)}) copy-start(bf16[16,64,64]{2,1,0:T(8,128)(2,1)} %param.16) | copy-start | bytes 393220
  19.7 58.7 %copy-start.1 = (bf16[16,64,256]{2,1,0:T(8,128)(2,1)S(1)}, bf16[16,64,256]{2,1,0:T(8,128)(2,1)}, u32[]{:S(2)}) copy-start(bf16[16,64,256]{2,1,0:T(8,128)(2,1)} %param.15) | copy-start | bytes 1572868
  20.0 58.6 %copy-start.3 = (f32[16,256]{1,0:T(8,128)S(1)}, f32[16,256]{1,0:T(8,128)}, u32[]{:S(2)}) copy-start(f32[16,256]{1,0:T(8,128)} %param.12) | copy-start | bytes 49156
  21.0 40.0 %collective-permute-start.3 = (bf16[40,64]{1,0:T(8,128)(2,1)S(1)}, bf16[40,64]{1,0:T(8,128)(2,1)S(1)}, u32[]{:S(2)}, u32[]{:S(2)}) collective-permute-start(bf16[40,64]{1,0:T(8,128)(2,1)S(1)} %pad_maximum_fusion.4), channel_id=1, source_target_pairs={{0,24},{4,28},{8,0},{12,4},{16,8},{20,12},{24,16},{28,20},{1,25},{... | collective-permute-start | bytes 15368 | tf_op jit(solution)/shard_map/ppermute | solution.py:85
  61.0 4.7 %collective-permute-start.4 = (bf16[80,64]{1,0:T(8,128)(2,1)S(1)}, bf16[80,64]{1,0:T(8,128)(2,1)S(1)}, u32[]{:S(2)}, u32[]{:S(2)}) collective-permute-start(bf16[80,64]{1,0:T(8,128)(2,1)S(1)} %pad_maximum_fusion), channel_id=1, source_target_pairs={{0,16},{4,20},{8,24},{12,28},{16,0},{20,4},{24,8},{28,12},{1,17},{... | collective-permute-start | bytes 30728 | tf_op jit(solution)/shard_map/ppermute | solution.py:85
  120.0 51.1 %collective-permute-start.5 = (bf16[16,256]{1,0:T(8,128)(2,1)S(1)}, bf16[16,256]{1,0:T(8,128)(2,1)S(1)}, u32[]{:S(2)}, u32[]{:S(2)}) collective-permute-start(bf16[16,256]{1,0:T(8,128)(2,1)S(1)} %fusion.55), channel_id=1, source_target_pairs={{4,0},{8,4},{12,8},{16,12},{20,16},{24,20},{28,24},{5,1},{9,5},{13... | collective-permute-start | bytes 24584 | tf_op jit(solution)/shard_map/ppermute | solution.py:12
  124.6 50.7 %collective-permute-start.6 = (f32[16,256]{1,0:T(8,128)S(1)}, f32[16,256]{1,0:T(8,128)S(1)}, u32[]{:S(2)}, u32[]{:S(2)}) collective-permute-start(f32[16,256]{1,0:T(8,128)S(1)} %slice.51), channel_id=1, source_target_pairs={{0,4},{4,8},{8,12},{12,16},{16,20},{20,24},{24,28},{1,5},{5,9},{9,... | collective-permute-start | bytes 49160 | tf_op jit(solution)/shard_map/ppermute | solution.py:12
  129.5 4.6 %collective-permute-start.7 = (bf16[20,64]{1,0:T(8,128)(2,1)S(1)}, bf16[20,64]{1,0:T(8,128)(2,1)S(1)}, u32[]{:S(2)}, u32[]{:S(2)}) collective-permute-start(bf16[20,64]{1,0:T(8,128)(2,1)S(1)} %get-tuple-element.22), channel_id=1, source_target_pairs={{0,28},{4,0},{8,4},{12,8},{16,12},{20,16},{24,20},{28,24},{1,29},{... | collective-permute-start | bytes 7688 | tf_op jit(solution)/shard_map/ppermute | solution.py:85
  134.1 37.0 %collective-permute-start.8 = (bf16[40,64]{1,0:T(8,128)(2,1)S(1)}, bf16[40,64]{1,0:T(8,128)(2,1)S(1)}, u32[]{:S(2)}, u32[]{:S(2)}) collective-permute-start(bf16[40,64]{1,0:T(8,128)(2,1)S(1)} %pad_maximum_fusion.5), channel_id=1, source_target_pairs={{0,24},{4,28},{8,0},{12,4},{16,8},{20,12},{24,16},{28,20},{1,25},{... | collective-permute-start | bytes 15368 | tf_op jit(solution)/shard_map/ppermute | solution.py:85
  171.1 4.7 %collective-permute-start.9 = (bf16[80,64]{1,0:T(8,128)(2,1)S(1)}, bf16[80,64]{1,0:T(8,128)(2,1)S(1)}, u32[]{:S(2)}, u32[]{:S(2)}) collective-permute-start(bf16[80,64]{1,0:T(8,128)(2,1)S(1)} %pad_maximum_fusion.1), channel_id=1, source_target_pairs={{0,16},{4,20},{8,24},{12,28},{16,0},{20,4},{24,8},{28,12},{1,17},{... | collective-permute-start | bytes 30728 | tf_op jit(solution)/shard_map/ppermute | solution.py:85
